TPU v7x, 256 devices: a whole 4x4x8 slice. The times are simulated.
256 devices in a mesh: dp: 128 (over x, y_lo, z, core), section: 2 (over y_hi).
Axes of the slice: x: 4, y: 4 (y_hi: 2, y_lo: 2; y = y_hi * 2 + y_lo), z: 8, core: 2. Of those that a mesh axis runs over, the one named last changes fastest.
Arguments:
- replay_rows: bfloat16 [65536, 4, 4, 128], P('dp'), may hold values from -6 to 6
- qvalues: bfloat16 [65536, 18], P('dp'), may hold values from -5 to 129
- target_logits: bfloat16 [65536, 18], P('dp'), may hold values from -8 to 258
- replay_owner: int32 [32768], P(('dp', 'section')), may hold values from 0 to 127, as said below
- replay_slot: int32 [32768], P(('dp', 'section')), may hold values from 0 to 511
- sample_actions: int32 [32768, 20], P(('dp', 'section')), may hold values from 0 to 17
- weights: bfloat16 [2, 147456], replicated, may hold values from -0.1875 to 0.1875
- head: bfloat16 [128, 18], replicated, may hold values from -0.5 to 0.5
- master: float32 [2, 147456], P('section', 'dp'), may hold values from -0.0012 to 0.0012
- moment_first: float32 [2, 147456], P('section', 'dp'), may hold values from -0.0021 to 0.0021
- moment_second: float32 [2, 147456], P('section', 'dp'), may hold values from 9.9e-14 to 1.01e-06
Outputs:
- adam_step: float32 [2, 147456], P('section', 'dp')
- new_weights: bfloat16 [2, 147456], replicated
Inputs may be any that keep to these rules, and one draw needn't show every extreme that they name: `replay_owner`: among the 128 rows of one learner device no shard is named more than 2 times; in every draw one shard is named exactly 2 times by every learner device.
All inputs are finite; a program needn't handle non-finite values.
Results may differ from a plain program's by a relative error of at most 0.013.
Values may be sent and summed in bfloat16 or wider, within the bound.
No kernel may reach another device: no remote copies, remote signals or barrier semaphores. Data moves between devices by JAX's collectives and lax.ppermute only.
A program may use at most 192 MiB of HBM per device.

v0:
```python
import jax
import jax.numpy as jnp
from jax import lax
from jax.sharding import PartitionSpec as P

constant_entropy_scale = 0.5
trust_weight = 0.5
beta_first = 0.9
beta_second = 0.999
epsilon = 1e-08
learn_rate = 0.0001


def tap_stack(field):
    grid_side = field.shape[1]
    padded_rows = jnp.pad(field, ((0, 0), (1, 1), (1, 1), (0, 0)))
    return jnp.concatenate(
        [
            padded_rows[:, shift_row : shift_row + grid_side, shift_col : shift_col + grid_side, :]
            for shift_row in range(3)
            for shift_col in range(3)
        ],
        axis=-1,
    )


def layer_grads(
    features,
    move_return_estimates,
    reference_policy_entries,
    actions,
    row_scale,
    w_first,
    second_weight,
    head,
):
    row_count, grid_side, _, channels = features.shape
    positions = row_count * grid_side * grid_side
    taps_first = tap_stack(features).reshape(positions, 9 * channels)
    hidden = jax.nn.relu(jnp.dot(taps_first, w_first, preferred_element_type=jnp.float32)).astype(
        jnp.bfloat16
    )
    taps_second = tap_stack(hidden.reshape(features.shape)).reshape(positions, 9 * channels)
    summed = features.reshape(positions, channels).astype(jnp.float32) + jnp.dot(
        taps_second, second_weight, preferred_element_type=jnp.float32
    )
    block_out = jax.nn.relu(summed).astype(jnp.bfloat16)
    averaged_embedding = jnp.mean(
        block_out.astype(jnp.float32).reshape(row_count, grid_side * grid_side, channels), axis=1
    ).astype(jnp.bfloat16)
    logits = reference_policy_entries.astype(jnp.float32) + jnp.dot(
        averaged_embedding, head, preferred_element_type=jnp.float32
    )
    policy = jax.nn.softmax(logits, axis=-1)
    prior = jax.nn.softmax(reference_policy_entries.astype(jnp.float32), axis=-1)
    selected_moves = (actions[:, :, None] == jnp.arange(head.shape[1])[None, None, :]).astype(
        jnp.float32
    )
    move_logit_matrix = (
        jnp.einsum("vlu,vu->vl", selected_moves, move_return_estimates.astype(jnp.float32))
        / constant_entropy_scale
    )
    sample_weight = jax.nn.softmax(move_logit_matrix, axis=-1)
    logit_grad = (
        (1.0 + trust_weight) * policy
        - jnp.einsum("nk,nka->na", sample_weight, selected_moves)
        - trust_weight * prior
    ) * row_scale[:, None]
    pooled_grad = jnp.dot(logit_grad, head.astype(jnp.float32).T, precision=lax.Precision.HIGHEST)
    spread = jnp.broadcast_to(
        (pooled_grad / (grid_side * grid_side))[:, None, :],
        (row_count, grid_side * grid_side, channels),
    ).reshape(positions, channels)
    out_grad = jnp.where(block_out > 0, spread, 0.0).astype(jnp.bfloat16)
    grad_second = lax.dot_general(
        taps_second, out_grad, (((0,), (0,)), ((), ())), preferred_element_type=jnp.float32
    )
    flipped = (
        second_weight.reshape(9, channels, channels)[::-1]
        .transpose(0, 2, 1)
        .reshape(9 * channels, channels)
    )
    taps_back = tap_stack(out_grad.reshape(features.shape)).reshape(positions, 9 * channels)
    hidden_grad = jnp.where(
        hidden > 0, jnp.dot(taps_back, flipped, preferred_element_type=jnp.float32), 0.0
    ).astype(jnp.bfloat16)
    grad_first = lax.dot_general(
        taps_first, hidden_grad, (((0,), (0,)), ((), ())), preferred_element_type=jnp.float32
    )
    return (grad_first, grad_second)


def per_device(
    replay_rows,
    qvalues,
    target_logits,
    replay_owner,
    replay_slot,
    sample_actions,
    weights,
    head,
    master,
    moment_first,
    moment_second,
):
    rows_dev = replay_owner.shape[0]
    owners = lax.axis_size("dp")
    capacity = 2 * rows_dev // owners
    learn_rows = rows_dev * owners * lax.axis_size("section")
    channels = replay_rows.shape[3]
    w_first = weights[0].reshape(9 * channels, channels)
    second_weight = weights[1].reshape(9 * channels, channels)
    row_order = jnp.arange(rows_dev, dtype=jnp.int32)
    earlier = (replay_owner[None, :] == replay_owner[:, None]) & (
        row_order[None, :] < row_order[:, None]
    )
    rank_within = jnp.sum(earlier.astype(jnp.int32), axis=1)
    slot_index = replay_owner * capacity + rank_within
    matches = slot_index[None, :] == jnp.arange(owners * capacity, dtype=jnp.int32)[:, None]
    occupied_entries = jnp.any(matches, axis=1)
    source = jnp.sum(jnp.where(matches, row_order[None, :], 0), axis=1)
    request = jnp.where(occupied_entries, jnp.take(replay_slot, source), -1).reshape(
        owners, capacity
    )
    row_index = jnp.maximum(
        lax.all_to_all(request, "dp", split_axis=0, concat_axis=0, tiled=True), 0
    )
    feature_slots = lax.all_to_all(
        jnp.take(replay_rows, row_index, axis=0), "dp", split_axis=0, concat_axis=0, tiled=True
    )
    qvalue_slots = lax.all_to_all(
        jnp.take(qvalues, row_index, axis=0), "dp", split_axis=0, concat_axis=0, tiled=True
    )
    prior_slots = lax.all_to_all(
        jnp.take(target_logits, row_index, axis=0), "dp", split_axis=0, concat_axis=0, tiled=True
    )
    features = jnp.take(
        feature_slots.reshape((owners * capacity,) + feature_slots.shape[2:]), slot_index, axis=0
    )
    move_return_estimates = jnp.take(
        qvalue_slots.reshape(owners * capacity, -1), slot_index, axis=0
    )
    reference_policy_entries = jnp.take(
        prior_slots.reshape(owners * capacity, -1), slot_index, axis=0
    )
    row_scale = jnp.full((rows_dev,), 1.0 / learn_rows, jnp.float32)
    grad_first, grad_second = layer_grads(
        features,
        move_return_estimates,
        reference_policy_entries,
        sample_actions,
        row_scale,
        w_first,
        second_weight,
        head,
    )
    loss_derivative = jnp.stack([grad_first.reshape(-1), grad_second.reshape(-1)])
    piece_len = loss_derivative.shape[1] // owners
    regrouped = (
        loss_derivative.reshape(2, owners, piece_len)
        .transpose(1, 0, 2)
        .reshape(2 * owners, piece_len)
    )
    owned_grad = lax.psum_scatter(regrouped, ("dp", "section"), scatter_dimension=0, tiled=True)
    first = beta_first * moment_first + (1.0 - beta_first) * owned_grad
    second = beta_second * moment_second + (1.0 - beta_second) * owned_grad * owned_grad
    adam_step = first / (jnp.sqrt(second) + epsilon)
    new_piece = (master - learn_rate * adam_step).astype(jnp.bfloat16)
    collected = lax.all_gather(new_piece, ("dp", "section"), axis=0, tiled=True)
    new_weights = (
        collected.reshape(owners, 2, piece_len).transpose(1, 0, 2).reshape(2, owners * piece_len)
    )
    return (adam_step, new_weights)


def solution(mesh):
    placed = (
        P("dp", None, None, None),
        P("dp", None),
        P("dp", None),
        P(("dp", "section")),
        P(("dp", "section")),
        P(("dp", "section"), None),
        P(),
        P(),
        P("section", "dp"),
        P("section", "dp"),
        P("section", "dp"),
    )
    return jax.shard_map(
        per_device, mesh=mesh, in_specs=placed, out_specs=(P("section", "dp"), P()), check_vma=False
    )
```

profile of v0, /device:TPU:1, one launch (start us, length us, event | category | flops | bytes accessed | tf_op | source)
XLA Modules:
  0.0 1061.1 jit_solution(8042441142103392493)
XLA Ops:
  9.4 1.9 gather_fusion
  12.1 14.8 %all-to-all-start = ((s32[128,1,2]{2,1,0:T(1,128)}), s32[128,1,2]{2,1,0:T(1,128)S(1)}, u32[]{:S(2)}, u32[]{:S(2)}) async-start(s32[128,1,2]{2,1,0:T(1,128)} %bitcast.3), calls=%async_computation | async-start | bytes 131072 | tf_op jit(solution)/shard_map/all_to_all | solution.py:126
  28.7 8.9 all-to-all-done
  40.5 5.8 all-to-all-start.3
  46.3 1.5 gather_fusion.1
  47.9 9.3 all-to-all-done.3
  57.2 5.8 all-to-all-start.2
  62.9 1.5 broadcast_select_fusion
  64.5 9.3 all-to-all-done.2
  73.7 5.8 all-to-all-start.1
  80.0 8.4 slice_reduce_fusion
  89.9 1.8 copy.42
  93.7 16.3 %all-to-all-done.1 = bf16[128,2,4,4,128]{4,3,2,1,0:T(4,128)(2,1)S(1)} async-done(((bf16[128,2,4,4,128]{4,3,2,1,0:T(4,128)(2,1)}), bf16[128,2,4,4,128]{4,3,2,1,0:T(4,128)(2,1)S(1)}, u32[]{:S(2)}, u32[]{:S(2)}) %all-to-all-start.1) | async-done | bytes 1048608 | tf_op jit(solution)/shard_map/all_to_all | solution.py:128
  111.0 2.3 gather_fusion.2
  117.0 1.2 fusion.9
  119.4 1.2 fusion.10
  123.9 8.5 reshape.203
  132.5 3.7 fusion.2
  136.2 1.7 pad_slice_fusion.8
  139.1 1.9 convert_reduce_fusion
  141.7 2.3 fusion.53
  144.0 1.2 stack.8
  145.1 1.8 pad_slice_fusion
  148.1 2.2 copy-done.7
  150.3 8.8 fusion.5
  159.1 1.2 stack.7
  161.3 1.9 reshape.212
  163.2 253.9 %all-reduce.6.cloned.1.call-done = f32[256,1152]{1,0:T(8,128)} async-done(((f32[256,1152]{1,0:T(8,128)}), f32[256,1152]{1,0:T(8,128)}) %all-reduce.6.cloned.1.call-update) | async-done | bytes 1179664
  417.1 1.4 convert_bitcast_fusion
  418.5 628.6 %all-gather = bf16[256,1,1152]{2,1,0:T(2,128)(2,1)S(1)} all-gather(bf16[1,1,1152]{2,1,0:T(2,128)(2,1)S(1)} %get-tuple-element.6), channel_id=1, replica_groups=mesh['dp'=128,'section'=2] {'dp','section'}, dimensions={0}, use_global_device_ids=true | all-gather | bytes 592128 | tf_op jit(solution)/shard_map/all_gather | solution.py:169
  1047.1 4.4 reduce.6
  1051.5 2.6 reshape.213
  (98 shorter events, 24.7 us)
Async XLA Ops:
  7.2 39.1 %copy-start = (bf16[512,4,4,128]{3,2,1,0:T(4,128)(2,1)S(1)}, bf16[512,4,4,128]{3,2,1,0:T(4,128)(2,1)}, u32[]{:S(2)}) copy-start(bf16[512,4,4,128]{3,2,1,0:T(4,128)(2,1)} %param.15) | copy-start | bytes 6291460
  12.1 25.4 %all-to-all-start = ((s32[128,1,2]{2,1,0:T(1,128)}), s32[128,1,2]{2,1,0:T(1,128)S(1)}, u32[]{:S(2)}, u32[]{:S(2)}) async-start(s32[128,1,2]{2,1,0:T(1,128)} %bitcast.3), calls=%async_computation | async-start | bytes 131072 | tf_op jit(solution)/shard_map/all_to_all | solution.py:126
  40.5 16.6 %all-to-all-start.3 = ((bf16[128,2,18]{2,1,0:T(2,128)(2,1)}), bf16[128,2,18]{2,1,0:T(2,128)(2,1)S(1)}, u32[]{:S(2)}, u32[]{:S(2)}) async-start(bf16[128,2,18]{2,1,0:T(2,128)(2,1)} %get-tuple-element.29), calls=%async_computation.3 | async-start | bytes 131072 | tf_op jit(solution)/shard_map/all_to_all | solution.py:131
  46.3 47.2 %copy-start.8 = (s32[128,20]{0,1:T(8,128)S(1)}, s32[128,20]{0,1:T(8,128)}, u32[]{:S(2)}) copy-start(s32[128,20]{0,1:T(8,128)} %param.20) | copy-start | bytes 30724
  57.2 16.6 %all-to-all-start.2 = ((bf16[128,2,18]{2,1,0:T(2,128)(2,1)}), bf16[128,2,18]{2,1,0:T(2,128)(2,1)S(1)}, u32[]{:S(2)}, u32[]{:S(2)}) async-start(bf16[128,2,18]{2,1,0:T(2,128)(2,1)} %get-tuple-element.28), calls=%async_computation.2 | async-start | bytes 131072 | tf_op jit(solution)/shard_map/all_to_all | solution.py:134
  73.7 36.3 %all-to-all-start.1 = ((bf16[128,2,4,4,128]{4,3,2,1,0:T(4,128)(2,1)}), bf16[128,2,4,4,128]{4,3,2,1,0:T(4,128)(2,1)S(1)}, u32[]{:S(2)}, u32[]{:S(2)}) async-start(bf16[128,2,4,4,128]{4,3,2,1,0:T(4,128)(2,1)} %broadcast_select_fusion), calls=%async_computation.1 | async-start | bytes 2097152 | tf_op jit(solution)/shard_map/all_to_all | solution.py:128
  79.5 337.5 %all-reduce.6.cloned.1.call-start = ((), (), s32[]{:S(2)}) async-start(), calls=%async_computation.4 | async-start | bytes 2359296
  88.4 0.7 copy-start.3
  110.0 1.0 copy-start.1
  123.9 8.5 copy-start.5
  136.2 2.4 copy-start.2
  137.9 1.2 copy-start.4
  139.1 1.9 copy-start.9
  146.9 3.4 copy-start.6
  148.1 2.2 copy-start.7
  159.1 258.0 %copy-start.10 = (f32[1,1152]{1,0:T(1,128)S(1)}, f32[1,1152]{1,0:T(1,128)}, u32[]{:S(2)}) copy-start(f32[1,1152]{1,0:T(1,128)} %param.23) | copy-start | bytes 13828
  159.1 258.0 %copy-start.11 = (f32[1,1152]{1,0:T(1,128)S(1)}, f32[1,1152]{1,0:T(1,128)}, u32[]{:S(2)}) copy-start(f32[1,1152]{1,0:T(1,128)} %param.25) | copy-start | bytes 13828
  159.1 258.0 %copy-start.12 = (f32[1,1152]{1,0:T(1,128)S(1)}, f32[1,1152]{1,0:T(1,128)}, u32[]{:S(2)}) copy-start(f32[1,1152]{1,0:T(1,128)} %param.24) | copy-start | bytes 13828
Sparse Core Ops, SparseCore 0:
  163.3 253.7 all-reduce.5
where the time goes:
time: 1070 us; the launch traced here: 1060 us
  blocking collectives  629 us (59%)
  waiting for transfers between devices  298 us (28%)
  local copies, waits for them, and re-layouts  57.9 us (5%)
  starting transfers between devices  32.2 us (3%)
  matrix products  17.1 us (2%)
  between operations  14.8 us (1%)
  other arithmetic  12.8 us (1%)
    all_gather x1, blocking collectives, per_device(): collected = lax.all_gather(new_piece, ('dp', 'section'), axis=0, tiled=True)  629 us
    unnamed x2, waiting for transfers between devices  254 us
  transfers between devices with their start and end apart: 5, of which 5 were waited for; matrix products, arithmetic and copies ran while one was open for 2% of the time, Pallas kernels for 0%

commit v1 on v0

--- a/solution.py
+++ b/solution.py
@@ -156,20 +156,18 @@
     )
     loss_derivative = jnp.stack([grad_first.reshape(-1), grad_second.reshape(-1)])
     piece_len = loss_derivative.shape[1] // owners
-    regrouped = (
-        loss_derivative.reshape(2, owners, piece_len)
-        .transpose(1, 0, 2)
-        .reshape(2 * owners, piece_len)
-    )
-    owned_grad = lax.psum_scatter(regrouped, ("dp", "section"), scatter_dimension=0, tiled=True)
+    layer = lax.axis_index("section")
+    offset = lax.axis_index("dp") * piece_len
+    summed = lax.psum(loss_derivative, ("dp", "section"))
+    owned_grad = lax.dynamic_slice(summed, (layer, offset), (1, piece_len))
     first = beta_first * moment_first + (1.0 - beta_first) * owned_grad
     second = beta_second * moment_second + (1.0 - beta_second) * owned_grad * owned_grad
     adam_step = first / (jnp.sqrt(second) + epsilon)
-    new_piece = (master - learn_rate * adam_step).astype(jnp.bfloat16)
-    collected = lax.all_gather(new_piece, ("dp", "section"), axis=0, tiled=True)
-    new_weights = (
-        collected.reshape(owners, 2, piece_len).transpose(1, 0, 2).reshape(2, owners * piece_len)
+    new_piece = (master - learn_rate * adam_step).astype(jnp.bfloat16).astype(jnp.float32)
+    placed = lax.dynamic_update_slice(
+        jnp.zeros(loss_derivative.shape, jnp.float32), new_piece, (layer, offset)
     )
+    new_weights = lax.psum(placed, ("dp", "section")).astype(jnp.bfloat16)
     return (adam_step, new_weights)
 
 

time: 1070 us -> 509 us (0.48)
  blocking collectives: 629 us -> 85.4 us
    all_gather x1 -> x0, blocking collectives: 629 us -> none  [per_device(): collected = lax.all_gather(new_piece, ('dp', 'section'), axis=0, tiled=True)]
    unnamed x2 -> x1, waiting for transfers between devices: 254 us -> 0.02 us
    psum x0 -> x1, waiting for transfers between devices: none -> 254 us  [per_device(): summed = lax.psum(loss_derivative, ('dp', 'section'))]
    psum x0 -> x1, blocking collectives: none -> 85.4 us  [per_device(): new_weights = lax.psum(placed, ('dp', 'section')).astype(jnp.bfloat16)]
  transfers between devices with their start and end apart: 5 -> 5, of which waited for: 5 -> 5; matrix products, arithmetic and copies ran while one was open for 2% -> 4% of each run, Pallas kernels for 0% -> 0%
where the time goes in v1:
time: 509 us; the launch traced here: 508 us
  waiting for transfers between devices  298 us (59%)
  blocking collectives  85.4 us (17%)
  local copies, waits for them, and re-layouts  50.7 us (10%)
  starting transfers between devices  32.2 us (6%)
  matrix products  16.4 us (3%)
  between operations  14.5 us (3%)
  other arithmetic  11.3 us (2%)
    psum x1, waiting for transfers between devices, per_device(): summed = lax.psum(loss_derivative, ('dp', 'section'))  254 us
    psum x1, blocking collectives, per_device(): new_weights = lax.psum(placed, ('dp', 'section')).astype(jnp.bfloat16)  85.4 us
    all_to_all x1, waiting for transfers between devices, per_device(): lax.all_to_all(jnp.take(replay_rows, row_index, axis=0), 'dp', split_axis...  16.4 us
    unnamed x50, local copies, waits for them, and re-layouts  15.7 us
    all_to_all x1, starting transfers between devices, per_device(): lax.all_to_all(request, 'dp', split_axis=0, concat_axis=0, tiled=True)  14.8 us
  transfers between devices with their start and end apart: 5, of which 5 were waited for; matrix products, arithmetic and copies ran while one was open for 4% of the time, Pallas kernels for 0%

profile of v1, /device:TPU:1, one launch (start us, length us, event | category | flops | bytes accessed | tf_op | source)
XLA Modules:
  0.0 508.3 jit_solution(2481217592914121581)
XLA Ops:
  9.4 1.9 gather_fusion
  12.1 14.8 %all-to-all-start = ((s32[128,1,2]{2,1,0:T(1,128)}), s32[128,1,2]{2,1,0:T(1,128)S(1)}, u32[]{:S(2)}, u32[]{:S(2)}) async-start(s32[128,1,2]{2,1,0:T(1,128)} %bitcast.3), calls=%async_computation | async-start | bytes 131072 | tf_op jit(solution)/shard_map/all_to_all | solution.py:126
  28.7 8.9 %all-to-all-done = s32[128,1,2]{2,1,0:T(1,128)S(1)} async-done(((s32[128,1,2]{2,1,0:T(1,128)}), s32[128,1,2]{2,1,0:T(1,128)S(1)}, u32[]{:S(2)}, u32[]{:S(2)}) %all-to-all-start) | async-done | bytes 1056 | tf_op jit(solution)/shard_map/all_to_all | solution.py:126
  40.5 5.8 %all-to-all-start.3 = ((bf16[128,2,18]{2,1,0:T(2,128)(2,1)}), bf16[128,2,18]{2,1,0:T(2,128)(2,1)S(1)}, u32[]{:S(2)}, u32[]{:S(2)}) async-start(bf16[128,2,18]{2,1,0:T(2,128)(2,1)} %get-tuple-element.29), calls=%async_computation.3 | async-start | bytes 131072 | tf_op jit(solution)/shard_map/all_to_all | solution.py:131
  46.3 1.5 gather_fusion.1
  47.9 9.3 %all-to-all-done.3 = bf16[128,2,18]{2,1,0:T(2,128)(2,1)S(1)} async-done(((bf16[128,2,18]{2,1,0:T(2,128)(2,1)}), bf16[128,2,18]{2,1,0:T(2,128)(2,1)S(1)}, u32[]{:S(2)}, u32[]{:S(2)}) %all-to-all-start.3) | async-done | bytes 9248 | tf_op jit(solution)/shard_map/all_to_all | solution.py:131
  57.2 5.8 %all-to-all-start.2 = ((bf16[128,2,18]{2,1,0:T(2,128)(2,1)}), bf16[128,2,18]{2,1,0:T(2,128)(2,1)S(1)}, u32[]{:S(2)}, u32[]{:S(2)}) async-start(bf16[128,2,18]{2,1,0:T(2,128)(2,1)} %get-tuple-element.28), calls=%async_computation.2 | async-start | bytes 131072 | tf_op jit(solution)/shard_map/all_to_all | solution.py:134
  62.9 1.5 broadcast_select_fusion
  64.5 9.3 %all-to-all-done.2 = bf16[128,2,18]{2,1,0:T(2,128)(2,1)S(1)} async-done(((bf16[128,2,18]{2,1,0:T(2,128)(2,1)}), bf16[128,2,18]{2,1,0:T(2,128)(2,1)S(1)}, u32[]{:S(2)}, u32[]{:S(2)}) %all-to-all-start.2) | async-done | bytes 9248 | tf_op jit(solution)/shard_map/all_to_all | solution.py:134
  73.7 5.8 %all-to-all-start.1 = ((bf16[128,2,4,4,128]{4,3,2,1,0:T(4,128)(2,1)}), bf16[128,2,4,4,128]{4,3,2,1,0:T(4,128)(2,1)S(1)}, u32[]{:S(2)}, u32[]{:S(2)}) async-start(bf16[128,2,4,4,128]{4,3,2,1,0:T(4,128)(2,1)} %broadcast_select_fusion), calls=%async_computation.1 | async-start | bytes 2097152 | tf_op jit(solution)/shard_map/all_to_all | solution.py:128
  80.0 8.3 %slice_reduce_fusion = (bf16[147456]{0:T(1024)(128)(2,1)S(1)}, bf16[147456]{0:T(1024)(128)(2,1)}) fusion(bf16[2,147456]{1,0:T(2,128)(2,1)} %param.21), kind=kLoop, calls=%fused_computation.46 | loop fusion | bytes 1179648 | tf_op jit(solution)/shard_map/slice | solution.py:112
  89.8 1.8 copy.38
  93.6 16.4 %all-to-all-done.1 = bf16[128,2,4,4,128]{4,3,2,1,0:T(4,128)(2,1)S(1)} async-done(((bf16[128,2,4,4,128]{4,3,2,1,0:T(4,128)(2,1)}), bf16[128,2,4,4,128]{4,3,2,1,0:T(4,128)(2,1)S(1)}, u32[]{:S(2)}, u32[]{:S(2)}) %all-to-all-start.1) | async-done | bytes 1048608 | tf_op jit(solution)/shard_map/all_to_all | solution.py:128
  111.0 2.3 gather_fusion.2
  113.6 1.1 fusion.6
  115.9 1.1 fusion.8
  117.0 1.2 fusion.9
  118.2 1.2 constant_dynamic-update-slice_fusion
  119.4 1.2 fusion.10
  122.8 1.1 fusion.13
  123.9 8.5 %reshape.189 = bf16[2048,1152]{1,0:T(8,128)(2,1)} reshape(bf16[128,4,4,1152]{3,2,1,0:T(4,128)(2,1)} %fusion.13) | data formatting | bytes 9437184 | tf_op jit(solution)/shard_map/reshape | solution.py:39
  132.5 3.7 fusion.2
  136.2 1.7 pad_slice_fusion.8
  139.1 2.0 convert_reduce_fusion
  141.7 1.4 fusion.53
  143.2 1.8 pad_slice_fusion
  146.1 2.2 copy-done.6
  148.3 8.8 %fusion.5 = f32[1152,128]{1,0:T(8,128)} fusion(bf16[2048,1152]{1,0:T(8,128)(2,1)} %reshape.189, bf16[2048,1152]{1,0:T(8,128)(2,1)} %copy-done.6, bf16[1152,128]{1,0:T(8,128)(2,1)S(1)} %bitcast.99, bf16[2048,128]{1,0:T(8,128)(2,1)S(1)} %fusion.2), kind=kOutput, calls=%fused_computation.45 | convolution fusion | flops 1208745984 | bytes 10846208 | tf_op jit(solution)/shard_map/dot_general | solution.py:87
  157.1 2.9 pad_maximum_fusion
  160.0 253.9 %all-reduce.6.cloned.1.call-done = f32[2,147456]{1,0:T(2,128)} async-done(((f32[2,147456]{1,0:T(2,128)}), f32[2,147456]{1,0:T(2,128)}) %all-reduce.6.cloned.1.call-update) | async-done | bytes 1179664 | tf_op jit(solution)/shard_map/psum | solution.py:161
  413.9 1.4 convert_convert_fusion
  416.0 85.4 %all-reduce.7 = bf16[2,147456]{1,0:T(2,128)(2,1)} all-reduce(f32[2,147456]{1,0:T(2,128)S(1)} %dynamic_update_slice.3), channel_id=1, replica_groups=mesh['dp'=128,'section'=2] {'dp','section'}, use_global_device_ids=true, to_apply=%region_11.14 | all-reduce | flops 294912 | bytes 1769472 | tf_op jit(solution)/shard_map/psum | solution.py:170
  (92 shorter events, 19.7 us)
Async XLA Ops:
  7.2 39.1 %copy-start = (bf16[512,4,4,128]{3,2,1,0:T(4,128)(2,1)S(1)}, bf16[512,4,4,128]{3,2,1,0:T(4,128)(2,1)}, u32[]{:S(2)}) copy-start(bf16[512,4,4,128]{3,2,1,0:T(4,128)(2,1)} %param.15) | copy-start | bytes 6291460
  12.1 25.4 %all-to-all-start = ((s32[128,1,2]{2,1,0:T(1,128)}), s32[128,1,2]{2,1,0:T(1,128)S(1)}, u32[]{:S(2)}, u32[]{:S(2)}) async-start(s32[128,1,2]{2,1,0:T(1,128)} %bitcast.3), calls=%async_computation | async-start | bytes 131072 | tf_op jit(solution)/shard_map/all_to_all | solution.py:126
  40.5 16.6 %all-to-all-start.3 = ((bf16[128,2,18]{2,1,0:T(2,128)(2,1)}), bf16[128,2,18]{2,1,0:T(2,128)(2,1)S(1)}, u32[]{:S(2)}, u32[]{:S(2)}) async-start(bf16[128,2,18]{2,1,0:T(2,128)(2,1)} %get-tuple-element.29), calls=%async_computation.3 | async-start | bytes 131072 | tf_op jit(solution)/shard_map/all_to_all | solution.py:131
  46.3 47.1 %copy-start.7 = (s32[128,20]{0,1:T(8,128)S(1)}, s32[128,20]{0,1:T(8,128)}, u32[]{:S(2)}) copy-start(s32[128,20]{0,1:T(8,128)} %param.20) | copy-start | bytes 30724
  57.2 16.6 %all-to-all-start.2 = ((bf16[128,2,18]{2,1,0:T(2,128)(2,1)}), bf16[128,2,18]{2,1,0:T(2,128)(2,1)S(1)}, u32[]{:S(2)}, u32[]{:S(2)}) async-start(bf16[128,2,18]{2,1,0:T(2,128)(2,1)} %get-tuple-element.28), calls=%async_computation.2 | async-start | bytes 131072 | tf_op jit(solution)/shard_map/all_to_all | solution.py:134
  73.7 36.3 %all-to-all-start.1 = ((bf16[128,2,4,4,128]{4,3,2,1,0:T(4,128)(2,1)}), bf16[128,2,4,4,128]{4,3,2,1,0:T(4,128)(2,1)S(1)}, u32[]{:S(2)}, u32[]{:S(2)}) async-start(bf16[128,2,4,4,128]{4,3,2,1,0:T(4,128)(2,1)} %broadcast_select_fusion), calls=%async_computation.1 | async-start | bytes 2097152 | tf_op jit(solution)/shard_map/all_to_all | solution.py:128
  79.5 334.3 %all-reduce.6.cloned.1.call-start = ((), (), s32[]{:S(2)}) async-start(), calls=%async_computation.4 | async-start | bytes 2359296 | tf_op jit(solution)/shard_map/psum | solution.py:161
  88.3 0.7 copy-start.2
  110.0 1.0 copy-start.1
  123.9 8.5 %copy-start.4 = (bf16[147456]{0:T(1024)(128)(2,1)S(1)}, bf16[147456]{0:T(1024)(128)(2,1)}, u32[]{:S(2)}) copy-start(bf16[147456]{0:T(1024)(128)(2,1)} %get-tuple-element.5) | copy-start | bytes 884740
  137.9 1.2 copy-start.3
  139.1 2.0 copy-start.8
  144.9 3.4 copy-start.5
  146.1 2.2 copy-start.6
  148.3 265.6 %copy-start.9 = (f32[1,1152]{1,0:T(1,128)S(1)}, f32[1,1152]{1,0:T(1,128)}, u32[]{:S(2)}) copy-start(f32[1,1152]{1,0:T(1,128)} %param.23) | copy-start | bytes 13828
  148.3 265.6 %copy-start.10 = (f32[1,1152]{1,0:T(1,128)S(1)}, f32[1,1152]{1,0:T(1,128)}, u32[]{:S(2)}) copy-start(f32[1,1152]{1,0:T(1,128)} %param.25) | copy-start | bytes 13828
  148.3 265.6 %copy-start.11 = (f32[1,1152]{1,0:T(1,128)S(1)}, f32[1,1152]{1,0:T(1,128)}, u32[]{:S(2)}) copy-start(f32[1,1152]{1,0:T(1,128)} %param.24) | copy-start | bytes 13828
Sparse Core Ops, SparseCore 0:
  160.1 253.7 all-reduce.5
